TPU v7x, 512 devices: a whole 4x4x16 slice. The times are simulated.
512 devices in a mesh: ctx: 64 (over x_hi, z, core), mp: 8 (over x_lo, y).
Axes of the slice: x: 4 (x_hi: 2, x_lo: 2; x = x_hi * 2 + x_lo), y: 4, z: 16, core: 2. Of those that a mesh axis runs over, the one named last changes fastest.
Arguments:
- queries: bfloat16 [4096, 8192], P('ctx', 'mp'), may hold values from -8 to 8
- keys: bfloat16 [4096, 1024], P('ctx', 'mp'), may hold values from -8 to 8
- values: bfloat16 [4096, 1024], P('ctx', 'mp'), may hold values from -6 to 6
- positions: int32 [4096], P('ctx'), may hold values from 0 to 4095, as said below
- x_normed: bfloat16 [4096, 8192], P('ctx', 'mp'), may hold values from -6 to 6
- w_gate: bfloat16 [8192, 16384], P('mp', 'ctx'), may hold values from -0.0625 to 0.0625
- w_up: bfloat16 [8192, 16384], P('mp', 'ctx'), may hold values from -0.0625 to 0.0625
Outputs:
- attended: bfloat16 [4096, 8192], P('ctx', 'mp')
- mlp_hidden: bfloat16 [4096, 16384], P('mp', 'ctx')
Inputs may be any that keep to these rules, and one draw needn't show every extreme that they name: `positions`: each position of 0 to 4095 appears exactly once.
All inputs are finite; a program needn't handle non-finite values.
Results may differ from a plain program's by a relative error of at most 0.02.
Values may be sent and summed in bfloat16 or wider, within the bound.
No kernel may reach another device: no remote copies, remote signals or barrier semaphores. Data moves between devices by JAX's collectives and lax.ppermute only.
A program may use at most 64 MiB of HBM per device.

v0:
```python
import jax
import jax.numpy as jnp
from jax import lax
from jax.sharding import Mesh, PartitionSpec as P

HEAD = 128
CTX = ("xh", "zz", "cc")


def per_device(queries, keys, values, positions, x_normed, w_gate, w_up):
    tok_rows = queries.shape[0]
    local_heads = queries.shape[1] // HEAD
    local_kv = keys.shape[1] // HEAD
    group = local_heads // local_kv
    scale = HEAD ** (-0.5)
    query_four = queries.reshape(tok_rows, local_kv, group, HEAD)
    top_run = jnp.full((local_kv, group, tok_rows), -1e30, jnp.float32)
    pos_hi = positions // 64
    pos_lo = positions - pos_hi * 64
    pos_cols = jnp.zeros((tok_rows, HEAD), jnp.bfloat16)
    pos_cols = pos_cols.at[:, 0].set(pos_hi.astype(jnp.bfloat16))
    pos_cols = pos_cols.at[:, 1].set(pos_lo.astype(jnp.bfloat16))
    kv_pack = jnp.concatenate((keys, values, pos_cols), axis=1)
    kv_all = lax.all_gather(kv_pack, CTX, axis=0, tiled=True)
    kv_width = keys.shape[1]
    k_piece = kv_all[:, :kv_width]
    v_piece = kv_all[:, kv_width : 2 * kv_width]
    pos_back = kv_all[:, 2 * kv_width :].astype(jnp.float32)
    k_pos = pos_back[:, 0] * 64.0 + pos_back[:, 1]
    q_pos = positions.astype(jnp.float32)
    count = k_piece.shape[0]
    k_three = k_piece.reshape(count, local_kv, HEAD)
    v_three = v_piece.reshape(count, local_kv, HEAD)
    scores = (
        jnp.einsum("tgjd,sgd->gjts", query_four, k_three, preferred_element_type=jnp.float32)
        * scale
    )
    visible = k_pos[None, :] <= q_pos[:, None]
    piece_top = jnp.max(jnp.where(visible, scores, jnp.float32(-1e30)), axis=-1)
    top_new = jnp.maximum(top_run, piece_top)
    weights = jnp.where(visible, jnp.exp(scores - top_new[..., None]), jnp.float32(0.0))
    total_new = jnp.sum(weights, axis=-1)
    mixed = jnp.einsum(
        "gjts,sgd->gjtd", weights.astype(jnp.bfloat16), v_three, preferred_element_type=jnp.float32
    )
    final_state = (top_new, total_new, mixed)
    top_run, total_run, accum = final_state
    normed = accum / total_run[..., None]
    attended = (
        jnp.transpose(normed, (2, 0, 1, 3))
        .reshape(tok_rows, local_heads * HEAD)
        .astype(jnp.bfloat16)
    )
    hidden_cols = w_gate.shape[1]
    both_weights = jnp.concatenate((w_gate, w_up), axis=1)
    pair_weights = lax.all_gather(both_weights, "cc", axis=1, tiled=True)
    x_half = lax.all_gather(x_normed, ("xh", "zz"), axis=0, tiled=True)
    block_terms = jnp.dot(x_half, pair_weights, preferred_element_type=jnp.float32).astype(
        jnp.bfloat16
    )
    summed = lax.psum_scatter(block_terms, "mp", scatter_dimension=0, tiled=True).astype(
        jnp.float32
    )
    width = 2 * hidden_cols
    per_core = []
    for owner in range(2):
        gate = summed[:, owner * width : owner * width + hidden_cols]
        up = summed[:, owner * width + hidden_cols : (owner + 1) * width]
        per_core.append((jax.nn.silu(gate) * up).astype(jnp.bfloat16))
    stacked = jnp.stack(per_core)
    core = lax.axis_index("cc")
    mine = stacked[core]
    other = stacked[1 - core]
    got = lax.ppermute(other, "cc", [(0, 1), (1, 0)])
    both = jnp.stack((mine, got))
    parity0 = both[core]
    parity1 = both[1 - core]
    rows = parity0.shape[0]
    chunk = tok_rows
    mlp_hidden = jnp.stack(
        (
            parity0.reshape(rows // chunk, chunk, hidden_cols),
            parity1.reshape(rows // chunk, chunk, hidden_cols),
        ),
        axis=1,
    ).reshape(2 * rows, hidden_cols)
    return (attended, mlp_hidden)


def solution(mesh):
    n_ctx = mesh.shape["ctx"]
    n_mp = mesh.shape["mp"]
    fine = Mesh(mesh.devices.reshape(2, n_ctx // 4, 2, n_mp), ("xh", "zz", "cc", "mp"))
    return jax.shard_map(
        per_device,
        mesh=fine,
        in_specs=(
            P(CTX, "mp"),
            P(CTX, "mp"),
            P(CTX, "mp"),
            P(CTX),
            P(CTX, "mp"),
            P("mp", CTX),
            P("mp", CTX),
        ),
        out_specs=(P(CTX, "mp"), P("mp", CTX)),
        check_vma=False,
    )
```

profile of v0, /device:TPU:1, one launch (start us, length us, event | category | flops | bytes accessed | tf_op | source)
XLA Modules:
  0.0 425.7 jit_solution(6835526162539869750)
XLA Ops:
  7.2 2.3 pad_maximum_fusion
  9.6 0.7 all-gather.8.cloned.1.call-update
  10.3 0.6 compare_reduce_fusion.1
  11.0 0.6 compare_reduce_fusion
  11.6 1.3 fusion.32
  12.9 0.7 fusion.31
  13.6 0.1 copy.18
  13.7 0.1 copy.19
  13.8 0.1 scatter.9
  14.0 1.4 pad_maximum_fusion.2
  15.4 22.5 %all-gather.6.cloned.1.call-done = bf16[1024,1024]{1,0:T(8,128)(2,1)} async-done(((bf16[1024,512]{1,0:T(8,128)(2,1)}), bf16[1024,1024]{1,0:T(8,128)(2,1)}) %all-gather.6.cloned.1.call-update) | async-done | bytes 2097168 | tf_op jit(solution)/shard_map/all_gather | solution.py:56
  37.9 157.3 %all-gather.8.cloned.1.call-done = bf16[2048,1024]{1,0:T(8,128)(2,1)} async-done(((bf16[64,1024]{1,0:T(8,128)(2,1)}), bf16[2048,1024]{1,0:T(8,128)(2,1)}) %all-gather.8.cloned.1.call-update) | async-done | bytes 4194320 | tf_op jit(solution)/shard_map/all_gather | solution.py:57
  195.2 9.3 %convert_bitcast_fusion = bf16[2048,1024]{0,1:T(8,128)(2,1)} fusion(bf16[1024,1024]{1,0:T(8,128)(2,1)} %all-gather.6.cloned.1.call-done, bf16[2048,1024]{1,0:T(8,128)(2,1)} %all-gather.8.cloned.1.call-done), kind=kOutput, calls=%fused_computation.8 | convolution fusion | flops 4297064448 | bytes 10485760 | tf_op jit(solution)/shard_map/dot_general | solution.py:58
  204.5 0.6 copy-done.3
  205.2 145.6 %all-gather.4.cloned.1.call-done = bf16[4096,384]{1,0:T(8,128)(2,1)} async-done(((bf16[64,384]{1,0:T(8,128)(2,1)}), bf16[4096,384]{1,0:T(8,128)(2,1)}) %all-gather.4.cloned.1.call-update) | async-done | bytes 3145744 | tf_op jit(solution)/shard_map/all_gather | solution.py:24
  350.8 1.5 slice_convert_fusion
  352.3 1.2 fusion.9
  353.5 0.2 broadcast_compare_fusion
  353.7 1.7 fusion
  355.4 3.2 copy-done.1
  358.6 2.4 fusion.3
  361.0 47.3 %reduce-scatter.2.cloned.1.call-done = bf16[256,1024]{0,1:T(8,128)(2,1)} async-done(((bf16[2048,1024]{0,1:T(8,128)(2,1)}), bf16[256,1024]{0,1:T(8,128)(2,1)}) %reduce-scatter.2.cloned.1.call-update) | async-done | bytes 524304 | tf_op jit(solution)/shard_map/reduce_scatter | solution.py:61
  408.3 1.1 convert_element_type.53
  409.4 0.2 fusion.30
  409.6 0.1 fusion.25
  409.7 2.6 collective-permute-start
  412.4 4.9 %fusion.16 = bf16[64,1,8,128]{3,0,2,1:T(8,128)(2,1)S(1)} fusion(f32[4096,64,8]{0,1,2:T(8,128)} %copy-done.1, f32[8,64]{1,0:T(8,128)S(1)} %broadcast_maximum_fusion, pred[64,4096]{1,0:T(8,128)(4,1)S(1)} %broadcast_compare_fusion, bf16[4096,384]{1,0:T(8,128)(2,1)S(1)} %copy-done.2, f32[8,64]{1,0:T(8,128)S(1)} %fusion.3), kind=kOutput, calls=%fused_computation.16 | convolution fusion | flops 545390592 | bytes 9838592 | tf_op jit(solution)/shard_map/gjts,sgd->gjtd/dot_general | solution.py:43
  417.4 0.7 copy.34
  418.1 0.1 fusion.23
  418.2 0.1 copy.23
  418.3 0.1 copy.22
  418.4 0.7 copy.24
  (19 shorter events, 0.4 us)
Async XLA Ops:
  7.2 346.5 %copy-start = (bf16[64,1024]{1,0:T(8,128)(2,1)S(1)}, bf16[64,1024]{1,0:T(8,128)(2,1)}, u32[]{:S(2)}) copy-start(bf16[64,1024]{1,0:T(8,128)(2,1)} %param.11) | copy-start | bytes 393220
  7.2 30.7 %all-gather.6.cloned.1.call-start = ((), (), s32[]{:S(2)}) async-start(), calls=%async_computation.2 | async-start | bytes 3145728 | tf_op jit(solution)/shard_map/all_gather | solution.py:56
  9.5 185.7 %all-gather.8.cloned.1.call-start = ((), (), s32[]{:S(2)}) async-start(), calls=%async_computation.3 | async-start | bytes 4325376 | tf_op jit(solution)/shard_map/all_gather | solution.py:57
  10.3 340.5 %all-gather.4.cloned.1.call-start = ((), (), s32[]{:S(2)}) async-start(), calls=%async_computation.1 | async-start | bytes 3194880 | tf_op jit(solution)/shard_map/all_gather | solution.py:24
  15.4 392.9 %reduce-scatter.2.cloned.1.call-start = ((), (), s32[]{:S(2)}) async-start(), calls=%async_computation.4 | async-start | bytes 4718592 | tf_op jit(solution)/shard_map/reduce_scatter | solution.py:61
  204.5 0.7 copy-start.3
  350.8 2.9 copy-start.2
  355.4 3.2 copy-start.1
  409.7 8.3 %collective-permute-start = (bf16[256,256]{0,1:T(8,128)(2,1)S(1)}, bf16[256,256]{0,1:T(8,128)(2,1)S(1)}, u32[]{:S(2)}, u32[]{:S(2)}) collective-permute-start(bf16[256,256]{0,1:T(8,128)(2,1)S(1)} %get-tuple-element.32), channel_id=1, source_target_pairs={{0,8},{8,0},{1,9},{9,1},{2,10},{10,2},{3,11},{11,3},{4,12},{12,4},... | collective-permute-start | bytes 393224 | tf_op jit(solution)/shard_map/ppermute | solution.py:74
Sparse Core Ops, SparseCore 0:
  10.1 27.7 all-gather.5
  41.0 154.1 all-gather.7
  199.1 151.6 all-gather.3
  353.5 54.7 reduce-scatter.1
where the time goes:
time: 426 us
  waiting for transfers between devices  373 us (88%)
  matrix products  15.9 us (4%)
  between operations  13.9 us (3%)
  other arithmetic  13.8 us (3%)
  local copies, waits for them, and re-layouts  5.9 us (1%)
    all_gather x1, waiting for transfers between devices, per_device(): x_half = lax.all_gather(x_normed, ('xh', 'zz'), axis=0, tiled=True)  157 us
    all_gather x1, waiting for transfers between devices, per_device(): kv_all = lax.all_gather(kv_pack, CTX, axis=0, tiled=True)  146 us
    reduce_scatter x1, waiting for transfers between devices, per_device(): lax.psum_scatter(block_terms, 'mp', scatter_dimension=0, tiled=True)  47.3 us
    all_gather x1, waiting for transfers between devices, per_device(): pair_weights = lax.all_gather(both_weights, 'cc', axis=1, tiled=True)  22.5 us
    dot_general x1, matrix products, per_device(): jnp.dot(x_half, pair_weights, preferred_element_type=jnp.float32)  9.31 us
  transfers between devices with their start and end apart: 5, of which 4 were waited for; matrix products, arithmetic and copies ran while one was open for 6% of the time, Pallas kernels for 0%

commit v1 on v0

--- a/solution.py
+++ b/solution.py
@@ -21,7 +21,14 @@
     pos_cols = pos_cols.at[:, 0].set(pos_hi.astype(jnp.bfloat16))
     pos_cols = pos_cols.at[:, 1].set(pos_lo.astype(jnp.bfloat16))
     kv_pack = jnp.concatenate((keys, values, pos_cols), axis=1)
-    kv_all = lax.all_gather(kv_pack, CTX, axis=0, tiled=True)
+
+    def push_ratios(block_in):
+        taken_in = tuple((block_in for _ in range(jax.lax.axis_size(CTX))))
+        f_now = jnp.stack(taken_in, axis=0)
+        q_next = jax.lax.all_to_all(f_now, CTX, 0, 0)
+        return jnp.concatenate(q_next, axis=0)
+
+    kv_all = push_ratios(kv_pack)
     kv_width = keys.shape[1]
     k_piece = kv_all[:, :kv_width]
     v_piece = kv_all[:, kv_width : 2 * kv_width]

time: 426 us -> 321 us (0.75)
  waiting for transfers between devices: 373 us -> 247 us
  starting transfers between devices: 2.79 us -> 22.4 us
    all_gather x1 -> x0, waiting for transfers between devices: 146 us -> none  [per_device(): kv_all = lax.all_gather(kv_pack, CTX, axis=0, tiled=True)]
    all_gather x1, waiting for transfers between devices: 157 us -> 191 us  [per_device(): x_half = lax.all_gather(x_normed, ('xh', 'zz'), axis=0, tiled=True)]
    all_gather x1, waiting for transfers between devices: 22.5 us -> 0.63 us  [per_device(): pair_weights = lax.all_gather(both_weights, 'cc', axis=1, tiled=True)]
    all_to_all x0 -> x1, starting transfers between devices: none -> 19.6 us  [push_ratios(): q_next = jax.lax.all_to_all(f_now, CTX, 0, 0)]
    reduce_scatter x1, waiting for transfers between devices: 47.3 us -> 55.2 us  [per_device(): lax.psum_scatter(block_terms, 'mp', scatter_dimension=0, tiled=True)]
  transfers between devices with their start and end apart: 5 -> 5, of which waited for: 4 -> 3; matrix products, arithmetic and copies ran while one was open for 6% -> 9% of each run, Pallas kernels for 0% -> 0%
where the time goes in v1:
time: 321 us; the launch traced here: 320 us
  waiting for transfers between devices  247 us (77%)
  starting transfers between devices  22.4 us (7%)
  matrix products  15.9 us (5%)
  between operations  13.9 us (4%)
  other arithmetic  11 us (3%)
  local copies, waits for them, and re-layouts  9.54 us (3%)
    all_gather x1, waiting for transfers between devices, per_device(): x_half = lax.all_gather(x_normed, ('xh', 'zz'), axis=0, tiled=True)  191 us
    reduce_scatter x1, waiting for transfers between devices, per_device(): lax.psum_scatter(block_terms, 'mp', scatter_dimension=0, tiled=True)  55.2 us
    all_to_all x1, starting transfers between devices, push_ratios(): q_next = jax.lax.all_to_all(f_now, CTX, 0, 0)  19.6 us
    dot_general x1, matrix products, per_device(): jnp.dot(x_half, pair_weights, preferred_element_type=jnp.float32)  9.33 us
  transfers between devices with their start and end apart: 5, of which 3 were waited for; matrix products, arithmetic and copies ran while one was open for 9% of the time, Pallas kernels for 0%

profile of v1, /device:TPU:1, one launch (start us, length us, event | category | flops | bytes accessed | tf_op | source)
XLA Modules:
  0.0 320.1 jit_solution(11882140696827384326)
XLA Ops:
  7.2 2.3 pad_maximum_fusion
  9.6 0.7 all-gather.5.cloned.1.call-update
  10.3 0.8 copy.21
  11.1 0.8 copy.20
  12.0 0.7 compare_reduce_fusion.1
  12.6 0.6 compare_reduce_fusion
  13.2 1.3 fusion.32
  14.6 0.7 fusion.31
  15.3 0.1 copy.22
  15.4 2.2 stack.14
  17.6 19.6 %all-to-all-start = ((bf16[64,64,384]{2,1,0:T(8,128)(2,1)}), bf16[64,64,384]{2,1,0:T(8,128)(2,1)S(1)}, u32[]{:S(2)}, u32[]{:S(2)}) async-start(bf16[64,64,384]{2,1,0:T(8,128)(2,1)} %stack.14), calls=%async_computation | async-start | bytes 6291456 | tf_op jit(solution)/shard_map/all_to_all | solution.py:28
  37.3 0.6 all-gather.3.cloned.1.call-done
  37.9 190.8 %all-gather.5.cloned.1.call-done = bf16[2048,1024]{1,0:T(8,128)(2,1)} async-done(((bf16[64,1024]{1,0:T(8,128)(2,1)}), bf16[2048,1024]{1,0:T(8,128)(2,1)}) %all-gather.5.cloned.1.call-update) | async-done | bytes 4194320 | tf_op jit(solution)/shard_map/all_gather | solution.py:64
  228.7 9.3 %convert_bitcast_fusion = bf16[2048,1024]{0,1:T(8,128)(2,1)} fusion(bf16[1024,1024]{1,0:T(8,128)(2,1)} %all-gather.3.cloned.1.call-done, bf16[2048,1024]{1,0:T(8,128)(2,1)} %all-gather.5.cloned.1.call-done), kind=kOutput, calls=%fused_computation.8 | convolution fusion | flops 4297064448 | bytes 10485760 | tf_op jit(solution)/shard_map/dot_general | solution.py:65
  238.0 0.6 copy-done.2
  238.7 0.1 slice_convert_fusion
  238.8 1.2 fusion.9
  240.0 0.2 broadcast_compare_fusion
  240.2 1.7 fusion
  241.9 3.2 %copy-done.1 = f32[4096,64,8]{0,1,2:T(8,128)} copy-done((f32[4096,64,8]{0,1,2:T(8,128)}, f32[4096,64,8]{0,1,2:T(8,128)S(1)}, u32[]{:S(2)}) %copy-start.1) | copy-done | bytes 8388632
  245.1 2.4 fusion.3
  247.6 55.2 %reduce-scatter.2.cloned.1.call-done = bf16[256,1024]{0,1:T(8,128)(2,1)} async-done(((bf16[2048,1024]{0,1:T(8,128)(2,1)}), bf16[256,1024]{0,1:T(8,128)(2,1)}) %reduce-scatter.2.cloned.1.call-update) | async-done | bytes 524304 | tf_op jit(solution)/shard_map/reduce_scatter | solution.py:68
  302.8 1.1 convert_element_type.53
  303.9 0.2 fusion.30
  304.1 0.1 fusion.25
  304.2 2.6 collective-permute-start
  306.8 4.9 %fusion.16 = bf16[64,1,8,128]{3,0,2,1:T(8,128)(2,1)S(1)} fusion(f32[4096,64,8]{0,1,2:T(8,128)} %copy-done.1, f32[8,64]{1,0:T(8,128)S(1)} %broadcast_maximum_fusion, pred[64,4096]{1,0:T(8,128)(4,1)S(1)} %broadcast_compare_fusion, bf16[4096,384]{1,0:T(8,128)(2,1)S(1)} %bitcast.81, f32[8,64]{1,0:T(8,128)S(1)} %fusion.3), kind=kOutput, calls=%fused_computation.16 | convolution fusion | flops 545390592 | bytes 9838592 | tf_op jit(solution)/shard_map/gjts,sgd->gjtd/dot_general | solution.py:50
  311.9 0.7 copy.37
  312.5 0.1 fusion.23
  312.6 0.1 copy.26
  312.8 0.1 copy.25
  312.9 0.7 copy.27
  (18 shorter events, 0.4 us)
Async XLA Ops:
  7.2 233.0 %copy-start = (bf16[64,1024]{1,0:T(8,128)(2,1)S(1)}, bf16[64,1024]{1,0:T(8,128)(2,1)}, u32[]{:S(2)}) copy-start(bf16[64,1024]{1,0:T(8,128)(2,1)} %param.11) | copy-start | bytes 393220
  7.2 30.7 %all-gather.3.cloned.1.call-start = ((), (), s32[]{:S(2)}) async-start(), calls=%async_computation.2 | async-start | bytes 3145728 | tf_op jit(solution)/shard_map/all_gather | solution.py:63
  9.5 219.1 %all-gather.5.cloned.1.call-start = ((), (), s32[]{:S(2)}) async-start(), calls=%async_computation.3 | async-start | bytes 4325376 | tf_op jit(solution)/shard_map/all_gather | solution.py:64
  17.6 221.1 %all-to-all-start = ((bf16[64,64,384]{2,1,0:T(8,128)(2,1)}), bf16[64,64,384]{2,1,0:T(8,128)(2,1)S(1)}, u32[]{:S(2)}, u32[]{:S(2)}) async-start(bf16[64,64,384]{2,1,0:T(8,128)(2,1)} %stack.14), calls=%async_computation | async-start | bytes 6291456 | tf_op jit(solution)/shard_map/all_to_all | solution.py:28
  37.2 265.6 %reduce-scatter.2.cloned.1.call-start = ((), (), s32[]{:S(2)}) async-start(), calls=%async_computation.4 | async-start | bytes 4718592 | tf_op jit(solution)/shard_map/reduce_scatter | solution.py:68
  238.0 0.7 copy-start.2
  241.9 3.2 %copy-start.1 = (f32[4096,64,8]{0,1,2:T(8,128)}, f32[4096,64,8]{0,1,2:T(8,128)S(1)}, u32[]{:S(2)}) copy-start(f32[4096,64,8]{0,1,2:T(8,128)S(1)} %get-tuple-element.35) | copy-start | bytes 25165828
  304.2 8.4 %collective-permute-start = (bf16[256,256]{0,1:T(8,128)(2,1)S(1)}, bf16[256,256]{0,1:T(8,128)(2,1)S(1)}, u32[]{:S(2)}, u32[]{:S(2)}) collective-permute-start(bf16[256,256]{0,1:T(8,128)(2,1)S(1)} %get-tuple-element.32), channel_id=1, source_target_pairs={{0,8},{8,0},{1,9},{9,1},{2,10},{10,2},{3,11},{11,3},{4,12},{12,4},... | collective-permute-start | bytes 393224 | tf_op jit(solution)/shard_map/ppermute | solution.py:81
Sparse Core Ops, SparseCore 0:
  10.1 27.7 all-gather.2
  41.0 187.6 all-gather.4
  238.2 64.5 reduce-scatter.1
